TPU v7x, 32 devices: a whole 2x2x4 slice. The times are simulated.
32 devices in a mesh: ta: 4 (over z), xyz: 8 (over y, x, core).
Axes of the slice: x: 2, y: 2, z: 4, core: 2. Of those that a mesh axis runs over, the one named last changes fastest.
Arguments:
- right_side: float32 [32, 4, 8, 4, 2, 2, 128], P(None, 'ta', 'xyz'), may hold values from -6 to 6
- coarse_links: bfloat16 [4, 8, 4, 2, 2, 9, 64, 128], P('ta', 'xyz'), may hold values from -3 to 3
- null_vectors: bfloat16 [4, 8, 4, 2, 2, 48, 128], P('ta', 'xyz'), may hold values from -0.29882812 to 0.29882812
- coarse_inverse: bfloat16 [4, 384, 384], P('ta', 'xyz'), may hold values from -2 to 2
Outputs:
- solution: float32 [32, 4, 8, 4, 2, 2, 128], P(None, 'ta', 'xyz')
- residual: float32 [32, 4, 8, 4, 2, 2, 128], P(None, 'ta', 'xyz')
All inputs are finite; a program needn't handle non-finite values.
Results may differ from a plain program's by a relative error of at most 0.0075.
Values may be sent and summed in bfloat16 or wider, within the bound.
No kernel may reach another device: no remote copies, remote signals or barrier semaphores. Data moves between devices by JAX's collectives and lax.ppermute only.
A program may use at most 64 MiB of HBM per device.

v0:
```python
import jax
import jax.numpy as jnp
from jax import lax
from jax.sharding import PartitionSpec as P

OMEGA = 0.4
EPS = 1e-06


def from_behind(x, axis, by):
    length = lax.axis_size(axis)
    return lax.ppermute(x, axis, [(i, (i + by) % length) for i in range(length)])


def with_halo(cells, sides, width):
    for axis, dim in sides:
        count = lax.axis_size(axis)
        head = lax.slice_in_dim(cells, 0, width, axis=dim)
        tail = lax.slice_in_dim(cells, cells.shape[dim] - width, cells.shape[dim], axis=dim)
        cells = jnp.concatenate(
            [
                lax.ppermute(tail, axis, [(i, (i + 1) % count) for i in range(count)]),
                cells,
                lax.ppermute(head, axis, [((i + 1) % count, i) for i in range(count)]),
            ],
            axis=dim,
        )
    return cells


def fetch_face(face, stride, extent, toward):
    nearby = from_behind(face, "xyz", -toward * stride)
    across = from_behind(face, "xyz", toward * stride * (extent - 1))
    coord = lax.axis_index("xyz") // stride % extent
    boundary = extent - 1 if toward > 0 else 0
    return jnp.where(coord == boundary, across, nearby)


def both_sides(lowered, which, stride, extent):
    length = lowered.shape[which]
    from_upper = fetch_face(lax.slice_in_dim(lowered, 0, 1, axis=which), stride, extent, 1)
    from_lower = fetch_face(
        lax.slice_in_dim(lowered, length - 1, length, axis=which), stride, extent, -1
    )
    upper = jnp.concatenate([lax.slice_in_dim(lowered, 1, length, axis=which), from_upper], which)
    lower = jnp.concatenate(
        [from_lower, lax.slice_in_dim(lowered, 0, length - 1, axis=which)], which
    )
    return (upper, lower)


def apply_links(coarse_links, lowered):
    blocks_total = lax.axis_size("xyz")
    across_x = 2 + 2 * min(blocks_total // 64, 1)
    across_z = blocks_total // (across_x * across_x)
    upper_x, lower_x = both_sides(lowered, 5, 1, across_x)
    upper_y, lower_y = both_sides(lowered, 4, across_x, across_x)
    upper_z, lower_z = both_sides(lowered, 3, across_x * across_x, across_z)
    padded = with_halo(lowered, (("ta", 1),), 1)
    upper_t = padded[:, 2:]
    lower_t = padded[:, :-2]
    stacked = jnp.stack(
        [lowered, upper_x, lower_x, upper_y, lower_y, upper_z, lower_z, upper_t, lower_t], 2
    )
    half_width = lowered.shape[-1] // 2
    real_part = stacked[..., :half_width]
    imag_part = stacked[..., half_width:]
    real_input = jnp.concatenate([real_part, -imag_part], -1)
    imag_input = jnp.concatenate([imag_part, real_part], -1)
    inputs = jnp.stack([real_input, imag_input], 0)
    result = jnp.einsum(
        "tbzyxdik,pntdbzyxk->pntbzyxi", coarse_links, inputs, preferred_element_type=jnp.float32
    )
    return jnp.concatenate([result[0], result[1]], -1)


def precondition(vector_in, null_vectors, coarse_inverse):
    lowered = vector_in.astype(jnp.bfloat16)
    coarse = jnp.einsum(
        "tbzyxjk,ntbzyxk->nj", null_vectors, lowered, preferred_element_type=jnp.float32
    ).astype(jnp.bfloat16)
    inverse_rows = coarse_inverse[0]
    correction = lax.dot_general(
        lax.all_gather(coarse, "xyz", axis=1, tiled=True),
        inverse_rows,
        (((1,), (1,)), ((), ())),
        preferred_element_type=jnp.float32,
    ).astype(jnp.bfloat16)
    prolonged = jnp.einsum(
        "tbzyxjk,nj->ntbzyxk", null_vectors, correction, preferred_element_type=jnp.float32
    )
    return OMEGA * vector_in + prolonged


def inner_rows(left_vec, right_vec):
    return jnp.sum(left_vec * right_vec, axis=(1, 2, 3, 4, 5, 6))


def scaled(weights, vector_in):
    return weights[:, None, None, None, None, None, None] * vector_in


def pair_products(image, residual):
    return lax.psum((inner_rows(image, image), inner_rows(image, residual)), ("ta", "xyz"))


def shards(right_side, coarse_links, null_vectors, coarse_inverse):
    residual = right_side
    direction_a = precondition(residual, null_vectors, coarse_inverse)
    image_a = apply_links(coarse_links, direction_a.astype(jnp.bfloat16))
    norm_a, correlation_a = pair_products(image_a, residual)
    step_a = correlation_a / (norm_a + EPS)
    solution = scaled(step_a, direction_a)
    residual = residual - scaled(step_a, image_a)
    direction_b = precondition(residual, null_vectors, coarse_inverse)
    image_b = apply_links(coarse_links, direction_b.astype(jnp.bfloat16))
    projection_sum = lax.psum(inner_rows(image_a, image_b), ("ta", "xyz"))
    beta_coef = projection_sum / (norm_a + EPS)
    image_b = image_b - scaled(beta_coef, image_a)
    direction_b = direction_b - scaled(beta_coef, direction_a)
    norm_b, correlation_b = pair_products(image_b, residual)
    step_b = correlation_b / (norm_b + EPS)
    solution = solution + scaled(step_b, direction_b)
    residual = residual - scaled(step_b, image_b)
    return (solution, residual)


def solution(mesh):
    in_specs = (
        P(None, "ta", "xyz", None, None, None, None),
        P("ta", "xyz", None, None, None, None, None, None),
        P("ta", "xyz", None, None, None, None, None),
        P("ta", "xyz", None),
    )
    out_specs = (
        P(None, "ta", "xyz", None, None, None, None),
        P(None, "ta", "xyz", None, None, None, None),
    )
    return jax.shard_map(shards, mesh=mesh, in_specs=in_specs, out_specs=out_specs, check_vma=False)
```

profile of v0, /device:TPU:0, one launch (start us, length us, event | category | flops | bytes accessed | tf_op | source)
XLA Modules:
  0.0 213.9 jit_solution(7676962154770344067)
XLA Ops:
  2.9 10.7 %all-gather = bf16[8,48,32]{1,2,0:T(8,128)(2,1)S(1)} all-gather(bf16[1,48,32]{1,2,0:T(8,128)(2,1)S(1)} %fusion.23), channel_id=1, replica_groups=mesh['ta'=4,'xyz'=8] {'xyz'}, dimensions={0}, use_global_device_ids=true | all-gather | bytes 27648 | tf_op jit(solution)/shard_map/all_gather | solution.py:84
  14.4 2.1 bitcast_dynamic-update-slice_fusion.5
  16.5 1.5 fusion.54
  18.0 1.5 collective-permute-start.7
  19.5 1.4 collective-permute-start.6
  20.9 1.5 fusion.55
  24.0 1.7 fusion.53
  25.7 1.4 fusion.52
  27.1 1.7 collective-permute-start.2
  32.6 3.6 %collective-permute-start.10 = (bf16[32,1,1,4,2,2,128]{6,0,5,4,3,2,1:T(8,128)(2,1)}, bf16[32,1,1,4,2,2,128]{6,0,5,4,3,2,1:T(8,128)(2,1)S(1)}, u32[]{:S(2)}, u32[]{:S(2)}) collective-permute-start(bf16[32,1,1,4,2,2,128]{6,0,5,4,3,2,1:T(8,128)(2,1)} %get-tuple-element.23), channel_id=1, source_target_pairs={{8,0},{16,8},{24,16},{0,24},{9,1},{17,9},{25,17},{1,25},{10,2},{18... | collective-permute-start | bytes 393224 | tf_op jit(solution)/shard_map/ppermute | solution.py:24
  37.1 1.5 collective-permute-start.9
  41.1 2.5 %collective-permute-done.8 = bf16[32,1,1,1,2,2,128]{6,0,5,4,3,2,1:T(8,128)(2,1)S(1)} collective-permute-done((bf16[32,1,1,1,2,2,128]{6,0,5,4,3,2,1:T(8,128)(2,1)S(1)}, bf16[32,1,1,1,2,2,128]{6,0,5,4,3,2,1:T(8,128)(2,1)S(1)}, u32[]{:S(2)}, u32[]{:S(2)}) %collective-permute-start.8) | collective-permute-done | bytes 32800 | tf_op jit(solution)/shard_map/ppermute | solution.py:12
  48.6 38.7 %all-reduce.1 = (f32[32]{0:T(128)S(1)}, f32[32]{0:T(128)S(1)}) all-reduce(f32[32]{0:T(128)S(1)} %get-tuple-element.11, f32[32]{0:T(128)S(1)} %get-tuple-element.10), channel_id=1, replica_groups=mesh['ta'=4,'xyz'=8] {'ta','xyz'}, use_global_device_ids=true, to_apply=%region_1.2 | all-reduce | flops 64 | bytes 512 | tf_op jit(solution)/shard_map/psum | solution.py:104
  88.3 10.0 %all-gather.1 = bf16[8,48,32]{1,2,0:T(8,128)(2,1)S(1)} all-gather(bf16[1,48,32]{1,2,0:T(8,128)(2,1)S(1)} %fusion.22), channel_id=1, replica_groups=mesh['ta'=4,'xyz'=8] {'xyz'}, dimensions={0}, use_global_device_ids=true | all-gather | bytes 27648 | tf_op jit(solution)/shard_map/all_gather | solution.py:84
  99.0 2.1 bitcast_dynamic-update-slice_fusion.2
  103.0 1.4 collective-permute-start.13
  106.8 2.4 %collective-permute-start.18 = (bf16[32,1,1,4,1,2,128]{6,0,5,4,3,2,1:T(8,128)(2,1)S(1)}, bf16[32,1,1,4,1,2,128]{6,0,5,4,3,2,1:T(8,128)(2,1)S(1)}, u32[]{:S(2)}, u32[]{:S(2)}) collective-permute-start(bf16[32,1,1,4,1,2,128]{6,0,5,4,3,2,1:T(8,128)(2,1)S(1)} %get-tuple-element.36), channel_id=1, source_target_pairs={{0,6},{1,7},{2,0},{3,1},{4,2},{5,3},{6,4},{7,5},{8,14},{9,15},{10,... | collective-permute-start | bytes 196616 | tf_op jit(solution)/shard_map/ppermute | solution.py:12
  109.2 2.6 %collective-permute-start.14 = (bf16[32,1,1,4,2,1,128]{6,0,5,4,3,2,1:T(8,128)(2,1)S(1)}, bf16[32,1,1,4,2,1,128]{6,0,5,4,3,2,1:T(8,128)(2,1)S(1)}, u32[]{:S(2)}, u32[]{:S(2)}) collective-permute-start(bf16[32,1,1,4,2,1,128]{6,0,5,4,3,2,1:T(8,128)(2,1)S(1)} %get-tuple-element.38), channel_id=1, source_target_pairs={{0,7},{1,0},{2,1},{3,2},{4,3},{5,4},{6,5},{7,6},{8,15},{9,8},{10,9... | collective-permute-start | bytes 196616 | tf_op jit(solution)/shard_map/ppermute | solution.py:12
  111.8 2.7 %collective-permute-done.15 = bf16[32,1,1,4,2,1,128]{6,0,5,4,3,2,1:T(8,128)(2,1)S(1)} collective-permute-done((bf16[32,1,1,4,2,1,128]{6,0,5,4,3,2,1:T(8,128)(2,1)S(1)}, bf16[32,1,1,4,2,1,128]{6,0,5,4,3,2,1:T(8,128)(2,1)S(1)}, u32[]{:S(2)}, u32[]{:S(2)}) %collective-permute-start.15) | collective-permute-done | bytes 65568 | tf_op jit(solution)/shard_map/ppermute | solution.py:12
  114.5 2.1 %collective-permute-start.22 = (bf16[32,1,1,4,2,2,128]{6,0,5,4,3,2,1:T(8,128)(2,1)S(1)}, bf16[32,1,1,4,2,2,128]{6,0,5,4,3,2,1:T(8,128)(2,1)S(1)}, u32[]{:S(2)}, u32[]{:S(2)}) collective-permute-start(bf16[32,1,1,4,2,2,128]{6,0,5,4,3,2,1:T(8,128)(2,1)S(1)} %copy-done.5), channel_id=1, source_target_pairs={{8,0},{16,8},{24,16},{0,24},{9,1},{17,9},{25,17},{1,25},{10,2},{18... | collective-permute-start | bytes 393224 | tf_op jit(solution)/shard_map/ppermute | solution.py:24
  116.7 2.0 collective-permute-start.23
  121.9 3.0 %collective-permute-done.20 = bf16[32,1,1,1,2,2,128]{6,0,5,4,3,2,1:T(8,128)(2,1)S(1)} collective-permute-done((bf16[32,1,1,1,2,2,128]{6,0,5,4,3,2,1:T(8,128)(2,1)S(1)}, bf16[32,1,1,1,2,2,128]{6,0,5,4,3,2,1:T(8,128)(2,1)S(1)}, u32[]{:S(2)}, u32[]{:S(2)}) %collective-permute-start.20) | collective-permute-done | bytes 32800 | tf_op jit(solution)/shard_map/ppermute | solution.py:12
  129.9 39.7 %psum.37 = f32[32]{0:T(128)S(1)} all-reduce(f32[32]{0:T(128)S(1)} %multiply_reduce_fusion.2), channel_id=1, replica_groups=mesh['ta'=4,'xyz'=8] {'ta','xyz'}, use_global_device_ids=true, to_apply=%region_5.6 | all-reduce | flops 32 | bytes 256 | tf_op jit(solution)/shard_map/psum | solution.py:117
  170.6 40.1 %all-reduce = (f32[32]{0:T(128)S(1)}, f32[32]{0:T(128)S(1)}) all-reduce(f32[32]{0:T(128)S(1)} %get-tuple-element.9, f32[32]{0:T(128)S(1)} %get-tuple-element.8), channel_id=1, replica_groups=mesh['ta'=4,'xyz'=8] {'ta','xyz'}, use_global_device_ids=true, to_apply=%region_7.8 | all-reduce | flops 64 | bytes 512 | tf_op jit(solution)/shard_map/psum | solution.py:104
  (115 shorter events, 34.7 us)
Async XLA Ops:
  18.0 21.6 %collective-permute-start.7 = (bf16[32,1,1,4,1,2,128]{6,0,5,4,3,2,1:T(8,128)(2,1)}, bf16[32,1,1,4,1,2,128]{6,0,5,4,3,2,1:T(8,128)(2,1)}, u32[]{:S(2)}, u32[]{:S(2)}) collective-permute-start(bf16[32,1,1,4,1,2,128]{6,0,5,4,3,2,1:T(8,128)(2,1)} %get-tuple-element.44), channel_id=1, source_target_pairs={{0,2},{1,3},{2,4},{3,5},{4,6},{5,7},{6,0},{7,1},{8,10},{9,11},{10,... | collective-permute-start | bytes 196616 | tf_op jit(solution)/shard_map/ppermute | solution.py:12
  19.5 20.7 %collective-permute-start.6 = (bf16[32,1,1,4,1,2,128]{6,0,5,4,3,2,1:T(8,128)(2,1)}, bf16[32,1,1,4,1,2,128]{6,0,5,4,3,2,1:T(8,128)(2,1)}, u32[]{:S(2)}, u32[]{:S(2)}) collective-permute-start(bf16[32,1,1,4,1,2,128]{6,0,5,4,3,2,1:T(8,128)(2,1)} %get-tuple-element.44), channel_id=1, source_target_pairs={{0,6},{1,7},{2,0},{3,1},{4,2},{5,3},{6,4},{7,5},{8,14},{9,15},{10,... | collective-permute-start | bytes 196616 | tf_op jit(solution)/shard_map/ppermute | solution.py:12
  22.5 4.6 %collective-permute-start.1 = (bf16[32,1,1,4,2,1,128]{6,0,5,4,3,2,1:T(8,128)(2,1)}, bf16[32,1,1,4,2,1,128]{6,0,5,4,3,2,1:T(8,128)(2,1)}, u32[]{:S(2)}, u32[]{:S(2)}) collective-permute-start(bf16[32,1,1,4,2,1,128]{6,0,5,4,3,2,1:T(8,128)(2,1)} %get-tuple-element.47), channel_id=1, source_target_pairs={{0,7},{1,0},{2,1},{3,2},{4,3},{5,4},{6,5},{7,6},{8,15},{9,8},{10,9... | collective-permute-start | bytes 196616 | tf_op jit(solution)/shard_map/ppermute | solution.py:12
  22.5 6.3 %collective-permute-start = (bf16[32,1,1,4,2,1,128]{6,0,5,4,3,2,1:T(8,128)(2,1)}, bf16[32,1,1,4,2,1,128]{6,0,5,4,3,2,1:T(8,128)(2,1)}, u32[]{:S(2)}, u32[]{:S(2)}) collective-permute-start(bf16[32,1,1,4,2,1,128]{6,0,5,4,3,2,1:T(8,128)(2,1)} %get-tuple-element.47), channel_id=1, source_target_pairs={{0,1},{1,2},{2,3},{3,4},{4,5},{5,6},{6,7},{7,0},{8,9},{9,10},{10,1... | collective-permute-start | bytes 196616 | tf_op jit(solution)/shard_map/ppermute | solution.py:12
  23.0 8.5 %collective-permute-start.3 = (bf16[32,1,1,4,2,1,128]{6,0,5,4,3,2,1:T(8,128)(2,1)}, bf16[32,1,1,4,2,1,128]{6,0,5,4,3,2,1:T(8,128)(2,1)}, u32[]{:S(2)}, u32[]{:S(2)}) collective-permute-start(bf16[32,1,1,4,2,1,128]{6,0,5,4,3,2,1:T(8,128)(2,1)} %get-tuple-element.46), channel_id=1, source_target_pairs={{0,1},{1,2},{2,3},{3,4},{4,5},{5,6},{6,7},{7,0},{8,9},{9,10},{10,1... | collective-permute-start | bytes 196616 | tf_op jit(solution)/shard_map/ppermute | solution.py:12
  27.1 5.5 %collective-permute-start.2 = (bf16[32,1,1,4,2,1,128]{6,0,5,4,3,2,1:T(8,128)(2,1)}, bf16[32,1,1,4,2,1,128]{6,0,5,4,3,2,1:T(8,128)(2,1)S(1)}, u32[]{:S(2)}, u32[]{:S(2)}) collective-permute-start(bf16[32,1,1,4,2,1,128]{6,0,5,4,3,2,1:T(8,128)(2,1)} %get-tuple-element.46), channel_id=1, source_target_pairs={{0,7},{1,0},{2,1},{3,2},{4,3},{5,4},{6,5},{7,6},{8,15},{9,8},{10,9... | collective-permute-start | bytes 196616 | tf_op jit(solution)/shard_map/ppermute | solution.py:12
  28.8 8.3 %collective-permute-start.5 = (bf16[32,1,1,4,1,2,128]{6,0,5,4,3,2,1:T(8,128)(2,1)}, bf16[32,1,1,4,1,2,128]{6,0,5,4,3,2,1:T(8,128)(2,1)S(1)}, u32[]{:S(2)}, u32[]{:S(2)}) collective-permute-start(bf16[32,1,1,4,1,2,128]{6,0,5,4,3,2,1:T(8,128)(2,1)} %get-tuple-element.45), channel_id=1, source_target_pairs={{0,6},{1,7},{2,0},{3,1},{4,2},{5,3},{6,4},{7,5},{8,14},{9,15},{10,... | collective-permute-start | bytes 196616 | tf_op jit(solution)/shard_map/ppermute | solution.py:12
  31.5 5.6 %collective-permute-start.4 = (bf16[32,1,1,4,1,2,128]{6,0,5,4,3,2,1:T(8,128)(2,1)}, bf16[32,1,1,4,1,2,128]{6,0,5,4,3,2,1:T(8,128)(2,1)S(1)}, u32[]{:S(2)}, u32[]{:S(2)}) collective-permute-start(bf16[32,1,1,4,1,2,128]{6,0,5,4,3,2,1:T(8,128)(2,1)} %get-tuple-element.45), channel_id=1, source_target_pairs={{0,2},{1,3},{2,4},{3,5},{4,6},{5,7},{6,0},{7,1},{8,10},{9,11},{10,... | collective-permute-start | bytes 196616 | tf_op jit(solution)/shard_map/ppermute | solution.py:12
  32.6 11.1 %collective-permute-start.10 = (bf16[32,1,1,4,2,2,128]{6,0,5,4,3,2,1:T(8,128)(2,1)}, bf16[32,1,1,4,2,2,128]{6,0,5,4,3,2,1:T(8,128)(2,1)S(1)}, u32[]{:S(2)}, u32[]{:S(2)}) collective-permute-start(bf16[32,1,1,4,2,2,128]{6,0,5,4,3,2,1:T(8,128)(2,1)} %get-tuple-element.23), channel_id=1, source_target_pairs={{8,0},{16,8},{24,16},{0,24},{9,1},{17,9},{25,17},{1,25},{10,2},{18... | collective-permute-start | bytes 393224 | tf_op jit(solution)/shard_map/ppermute | solution.py:24
  37.1 7.1 %collective-permute-start.11 = (bf16[32,1,1,4,2,2,128]{6,0,5,4,3,2,1:T(8,128)(2,1)}, bf16[32,1,1,4,2,2,128]{6,0,5,4,3,2,1:T(8,128)(2,1)S(1)}, u32[]{:S(2)}, u32[]{:S(2)}) collective-permute-start(bf16[32,1,1,4,2,2,128]{6,0,5,4,3,2,1:T(8,128)(2,1)} %get-tuple-element.23), channel_id=1, source_target_pairs={{0,8},{8,16},{16,24},{24,0},{1,9},{9,17},{17,25},{25,1},{2,10},{10... | collective-permute-start | bytes 393224 | tf_op jit(solution)/shard_map/ppermute | solution.py:22
  37.1 6.5 %collective-permute-start.9 = (bf16[32,1,1,1,2,2,128]{6,0,5,4,3,2,1:T(8,128)(2,1)}, bf16[32,1,1,1,2,2,128]{6,0,5,4,3,2,1:T(8,128)(2,1)S(1)}, u32[]{:S(2)}, u32[]{:S(2)}) collective-permute-start(bf16[32,1,1,1,2,2,128]{6,0,5,4,3,2,1:T(8,128)(2,1)} %get-tuple-element.40), channel_id=1, source_target_pairs={{0,4},{1,5},{2,6},{3,7},{4,0},{5,1},{6,2},{7,3},{8,12},{9,13},{10,... | collective-permute-start | bytes 98312 | tf_op jit(solution)/shard_map/ppermute | solution.py:12
  39.6 4.0 %collective-permute-start.8 = (bf16[32,1,1,1,2,2,128]{6,0,5,4,3,2,1:T(8,128)(2,1)S(1)}, bf16[32,1,1,1,2,2,128]{6,0,5,4,3,2,1:T(8,128)(2,1)S(1)}, u32[]{:S(2)}, u32[]{:S(2)}) collective-permute-start(bf16[32,1,1,1,2,2,128]{6,0,5,4,3,2,1:T(8,128)(2,1)S(1)} %copy-done.10), channel_id=1, source_target_pairs={{0,4},{1,5},{2,6},{3,7},{4,0},{5,1},{6,2},{7,3},{8,12},{9,13},{10,... | collective-permute-start | bytes 98312 | tf_op jit(solution)/shard_map/ppermute | solution.py:12
  103.0 6.3 %collective-permute-start.13 = (bf16[32,1,1,4,2,1,128]{6,0,5,4,3,2,1:T(8,128)(2,1)S(1)}, bf16[32,1,1,4,2,1,128]{6,0,5,4,3,2,1:T(8,128)(2,1)S(1)}, u32[]{:S(2)}, u32[]{:S(2)}) collective-permute-start(bf16[32,1,1,4,2,1,128]{6,0,5,4,3,2,1:T(8,128)(2,1)S(1)} %get-tuple-element.39), channel_id=1, source_target_pairs={{0,7},{1,0},{2,1},{3,2},{4,3},{5,4},{6,5},{7,6},{8,15},{9,8},{10,9... | collective-permute-start | bytes 196616 | tf_op jit(solution)/shard_map/ppermute | solution.py:12
  104.4 7.4 %collective-permute-start.12 = (bf16[32,1,1,4,2,1,128]{6,0,5,4,3,2,1:T(8,128)(2,1)S(1)}, bf16[32,1,1,4,2,1,128]{6,0,5,4,3,2,1:T(8,128)(2,1)S(1)}, u32[]{:S(2)}, u32[]{:S(2)}) collective-permute-start(bf16[32,1,1,4,2,1,128]{6,0,5,4,3,2,1:T(8,128)(2,1)S(1)} %get-tuple-element.39), channel_id=1, source_target_pairs={{0,1},{1,2},{2,3},{3,4},{4,5},{5,6},{6,7},{7,0},{8,9},{9,10},{10,1... | collective-permute-start | bytes 196616 | tf_op jit(solution)/shard_map/ppermute | solution.py:12
  106.2 14.8 %collective-permute-start.19 = (bf16[32,1,1,4,1,2,128]{6,0,5,4,3,2,1:T(8,128)(2,1)S(1)}, bf16[32,1,1,4,1,2,128]{6,0,5,4,3,2,1:T(8,128)(2,1)S(1)}, u32[]{:S(2)}, u32[]{:S(2)}) collective-permute-start(bf16[32,1,1,4,1,2,128]{6,0,5,4,3,2,1:T(8,128)(2,1)S(1)} %get-tuple-element.36), channel_id=1, source_target_pairs={{0,2},{1,3},{2,4},{3,5},{4,6},{5,7},{6,0},{7,1},{8,10},{9,11},{10,... | collective-permute-start | bytes 196616 | tf_op jit(solution)/shard_map/ppermute | solution.py:12
  106.8 15.1 %collective-permute-start.18 = (bf16[32,1,1,4,1,2,128]{6,0,5,4,3,2,1:T(8,128)(2,1)S(1)}, bf16[32,1,1,4,1,2,128]{6,0,5,4,3,2,1:T(8,128)(2,1)S(1)}, u32[]{:S(2)}, u32[]{:S(2)}) collective-permute-start(bf16[32,1,1,4,1,2,128]{6,0,5,4,3,2,1:T(8,128)(2,1)S(1)} %get-tuple-element.36), channel_id=1, source_target_pairs={{0,6},{1,7},{2,0},{3,1},{4,2},{5,3},{6,4},{7,5},{8,14},{9,15},{10,... | collective-permute-start | bytes 196616 | tf_op jit(solution)/shard_map/ppermute | solution.py:12
  109.2 5.4 %collective-permute-start.15 = (bf16[32,1,1,4,2,1,128]{6,0,5,4,3,2,1:T(8,128)(2,1)S(1)}, bf16[32,1,1,4,2,1,128]{6,0,5,4,3,2,1:T(8,128)(2,1)S(1)}, u32[]{:S(2)}, u32[]{:S(2)}) collective-permute-start(bf16[32,1,1,4,2,1,128]{6,0,5,4,3,2,1:T(8,128)(2,1)S(1)} %get-tuple-element.38), channel_id=1, source_target_pairs={{0,1},{1,2},{2,3},{3,4},{4,5},{5,6},{6,7},{7,0},{8,9},{9,10},{10,1... | collective-permute-start | bytes 196616 | tf_op jit(solution)/shard_map/ppermute | solution.py:12
  109.2 5.3 %collective-permute-start.14 = (bf16[32,1,1,4,2,1,128]{6,0,5,4,3,2,1:T(8,128)(2,1)S(1)}, bf16[32,1,1,4,2,1,128]{6,0,5,4,3,2,1:T(8,128)(2,1)S(1)}, u32[]{:S(2)}, u32[]{:S(2)}) collective-permute-start(bf16[32,1,1,4,2,1,128]{6,0,5,4,3,2,1:T(8,128)(2,1)S(1)} %get-tuple-element.38), channel_id=1, source_target_pairs={{0,7},{1,0},{2,1},{3,2},{4,3},{5,4},{6,5},{7,6},{8,15},{9,8},{10,9... | collective-permute-start | bytes 196616 | tf_op jit(solution)/shard_map/ppermute | solution.py:12
  111.8 4.9 %collective-permute-start.17 = (bf16[32,1,1,4,1,2,128]{6,0,5,4,3,2,1:T(8,128)(2,1)S(1)}, bf16[32,1,1,4,1,2,128]{6,0,5,4,3,2,1:T(8,128)(2,1)S(1)}, u32[]{:S(2)}, u32[]{:S(2)}) collective-permute-start(bf16[32,1,1,4,1,2,128]{6,0,5,4,3,2,1:T(8,128)(2,1)S(1)} %get-tuple-element.37), channel_id=1, source_target_pairs={{0,6},{1,7},{2,0},{3,1},{4,2},{5,3},{6,4},{7,5},{8,14},{9,15},{10,... | collective-permute-start | bytes 196616 | tf_op jit(solution)/shard_map/ppermute | solution.py:12
  114.5 5.2 %collective-permute-start.16 = (bf16[32,1,1,4,1,2,128]{6,0,5,4,3,2,1:T(8,128)(2,1)S(1)}, bf16[32,1,1,4,1,2,128]{6,0,5,4,3,2,1:T(8,128)(2,1)S(1)}, u32[]{:S(2)}, u32[]{:S(2)}) collective-permute-start(bf16[32,1,1,4,1,2,128]{6,0,5,4,3,2,1:T(8,128)(2,1)S(1)} %get-tuple-element.37), channel_id=1, source_target_pairs={{0,2},{1,3},{2,4},{3,5},{4,6},{5,7},{6,0},{7,1},{8,10},{9,11},{10,... | collective-permute-start | bytes 196616 | tf_op jit(solution)/shard_map/ppermute | solution.py:12
  114.5 10.5 %collective-permute-start.22 = (bf16[32,1,1,4,2,2,128]{6,0,5,4,3,2,1:T(8,128)(2,1)S(1)}, bf16[32,1,1,4,2,2,128]{6,0,5,4,3,2,1:T(8,128)(2,1)S(1)}, u32[]{:S(2)}, u32[]{:S(2)}) collective-permute-start(bf16[32,1,1,4,2,2,128]{6,0,5,4,3,2,1:T(8,128)(2,1)S(1)} %copy-done.5), channel_id=1, source_target_pairs={{8,0},{16,8},{24,16},{0,24},{9,1},{17,9},{25,17},{1,25},{10,2},{18... | collective-permute-start | bytes 393224 | tf_op jit(solution)/shard_map/ppermute | solution.py:24
  116.7 8.3 %collective-permute-start.23 = (bf16[32,1,1,4,2,2,128]{6,0,5,4,3,2,1:T(8,128)(2,1)S(1)}, bf16[32,1,1,4,2,2,128]{6,0,5,4,3,2,1:T(8,128)(2,1)S(1)}, u32[]{:S(2)}, u32[]{:S(2)}) collective-permute-start(bf16[32,1,1,4,2,2,128]{6,0,5,4,3,2,1:T(8,128)(2,1)S(1)} %copy-done.5), channel_id=1, source_target_pairs={{0,8},{8,16},{16,24},{24,0},{1,9},{9,17},{17,25},{25,1},{2,10},{10... | collective-permute-start | bytes 393224 | tf_op jit(solution)/shard_map/ppermute | solution.py:22
  119.7 5.3 %collective-permute-start.21 = (bf16[32,1,1,1,2,2,128]{6,0,5,4,3,2,1:T(8,128)(2,1)S(1)}, bf16[32,1,1,1,2,2,128]{6,0,5,4,3,2,1:T(8,128)(2,1)S(1)}, u32[]{:S(2)}, u32[]{:S(2)}) collective-permute-start(bf16[32,1,1,1,2,2,128]{6,0,5,4,3,2,1:T(8,128)(2,1)S(1)} %get-tuple-element.32), channel_id=1, source_target_pairs={{0,4},{1,5},{2,6},{3,7},{4,0},{5,1},{6,2},{7,3},{8,12},{9,13},{10,... | collective-permute-start | bytes 98312 | tf_op jit(solution)/shard_map/ppermute | solution.py:12
  121.0 4.0 %collective-permute-start.20 = (bf16[32,1,1,1,2,2,128]{6,0,5,4,3,2,1:T(8,128)(2,1)S(1)}, bf16[32,1,1,1,2,2,128]{6,0,5,4,3,2,1:T(8,128)(2,1)S(1)}, u32[]{:S(2)}, u32[]{:S(2)}) collective-permute-start(bf16[32,1,1,1,2,2,128]{6,0,5,4,3,2,1:T(8,128)(2,1)S(1)} %get-tuple-element.33), channel_id=1, source_target_pairs={{0,4},{1,5},{2,6},{3,7},{4,0},{5,1},{6,2},{7,3},{8,12},{9,13},{10,... | collective-permute-start | bytes 98312 | tf_op jit(solution)/shard_map/ppermute | solution.py:12
  (11 other events, 252.8 us)
where the time goes:
time: 215 us; the launch traced here: 214 us
  blocking collectives  139 us (65%)
  starting transfers between devices  27.3 us (13%)
  local copies, waits for them, and re-layouts  16.4 us (8%)
  other arithmetic  12.9 us (6%)
  waiting for transfers between devices  9.75 us (5%)
  matrix products  7.22 us (3%)
    psum x2, blocking collectives, pair_products(): lax.psum((inner_rows(image, image), inner_rows(image, residual)), ('ta',...  78.8 us
    psum x1, blocking collectives, shards(): projection_sum = lax.psum(inner_rows(image_a, image_b), ('ta', 'xyz'))  39.7 us
    all_gather x2, blocking collectives, precondition(): lax.all_gather(coarse, 'xyz', axis=1, tiled=True)  20.7 us
    ppermute x20, starting transfers between devices, from_behind(): lax.ppermute(x, axis, [(i, (i + by) % length) for i in range(length)])  19.5 us
    ppermute x20, waiting for transfers between devices, from_behind(): lax.ppermute(x, axis, [(i, (i + by) % length) for i in range(length)])  9.27 us
    ppermute x2, starting transfers between devices, with_halo(): lax.ppermute(head, axis, [((i + 1) % count, i) for i in range(count)])  5.75 us
    unnamed x28, local copies, waits for them, and re-layouts  5.09 us
    slice x4, local copies, waits for them, and re-layouts, both_sides(): lax.slice_in_dim(lowered, 1, length, axis=which)  4.87 us
  transfers between devices with their start and end apart: 24, of which 5 were waited for; matrix products, arithmetic and copies ran while one was open for 5% of the time, Pallas kernels for 0%

commit v1 on v0

--- a/solution.py
+++ b/solution.py
@@ -114,7 +114,8 @@
     residual = residual - scaled(step_a, image_a)
     direction_b = precondition(residual, null_vectors, coarse_inverse)
     image_b = apply_links(coarse_links, direction_b.astype(jnp.bfloat16))
-    projection_sum = lax.psum(inner_rows(image_a, image_b), ("ta", "xyz"))
+    half = lax.psum(inner_rows(image_a, image_b), "xyz")
+    projection_sum = lax.psum(half, "ta")
     beta_coef = projection_sum / (norm_a + EPS)
     image_b = image_b - scaled(beta_coef, image_a)
     direction_b = direction_b - scaled(beta_coef, direction_a)

time: 215 us -> 196 us (0.912)
  blocking collectives: 139 us -> 120 us
    psum x1 -> x2, blocking collectives: 39.7 us -> 23.2 us  [the longest x1 12.8 us: shards(): half = lax.psum(inner_rows(image_a, image_b), 'xyz')]
    psum x2, blocking collectives: 78.8 us -> 76.2 us  [pair_products(): lax.psum((inner_rows(image, image), inner_rows(image, residual)), ('ta',...]
  transfers between devices with their start and end apart: 24 -> 24, of which waited for: 5 -> 5; matrix products, arithmetic and copies ran while one was open for 5% -> 6% of each run, Pallas kernels for 0% -> 0%
where the time goes in v1:
time: 196 us; the launch traced here: 195 us
  blocking collectives  120 us (61%)
  starting transfers between devices  27.3 us (14%)
  local copies, waits for them, and re-layouts  16.4 us (8%)
  other arithmetic  12.9 us (7%)
  waiting for transfers between devices  9.75 us (5%)
  matrix products  7.22 us (4%)
    psum x2, blocking collectives, pair_products(): lax.psum((inner_rows(image, image), inner_rows(image, residual)), ('ta',...  76.2 us
    all_gather x2, blocking collectives, precondition(): lax.all_gather(coarse, 'xyz', axis=1, tiled=True)  20.7 us
    ppermute x20, starting transfers between devices, from_behind(): lax.ppermute(x, axis, [(i, (i + by) % length) for i in range(length)])  19.5 us
    psum x1, blocking collectives, shards(): half = lax.psum(inner_rows(image_a, image_b), 'xyz')  12.8 us
    psum x1, blocking collectives, shards(): projection_sum = lax.psum(half, 'ta')  10.5 us
    ppermute x20, waiting for transfers between devices, from_behind(): lax.ppermute(x, axis, [(i, (i + by) % length) for i in range(length)])  9.26 us
    ppermute x2, starting transfers between devices, with_halo(): lax.ppermute(head, axis, [((i + 1) % count, i) for i in range(count)])  5.78 us
    unnamed x28, local copies, waits for them, and re-layouts  5.1 us
  transfers between devices with their start and end apart: 24, of which 5 were waited for; matrix products, arithmetic and copies ran while one was open for 6% of the time, Pallas kernels for 0%

profile of v1, /device:TPU:0, one launch (start us, length us, event | category | flops | bytes accessed | tf_op | source)
XLA Modules:
  0.0 194.9 jit_solution(15306928956577903759)
XLA Ops:
  2.9 10.7 %all-gather = bf16[8,48,32]{1,2,0:T(8,128)(2,1)S(1)} all-gather(bf16[1,48,32]{1,2,0:T(8,128)(2,1)S(1)} %fusion.23), channel_id=1, replica_groups=mesh['ta'=4,'xyz'=8] {'xyz'}, dimensions={0}, use_global_device_ids=true | all-gather | bytes 27648 | tf_op jit(solution)/shard_map/all_gather | solution.py:84
  14.4 2.1 %bitcast_dynamic-update-slice_fusion.5 = (bf16[32,1,9,1,4,2,2,128]{7,0,6,5,4,3,2,1:T(8,128)(2,1)S(1)}, bf16[32,1,1,4,2,2,128]{6,0,5,4,3,2,1:T(8,128)(2,1)}, f32[32,1,1,4,2,2,128]{6,0,5,4,3,2,1:T(8,128)}) fusion(bf16[1,1,4,2,2,48,128]{6,5,4,3,2,1,0:T(8,128)(2,1)} %param.6, bf16[384,32]{0,1:T(8,128)(2,1)} %reshape.330, bf16[1,48,384]{2,1,0:T(8,128)(2,1)} %param.7, ...), kind=kOutput, calls=%fused_computation.76 | convolution fusion | flops 7669247 | bytes 1044480 | tf_op jit(solution)/shard_map/tbzyxjk,nj->ntbzyxk/dot_general | solution.py:89
  16.5 1.5 fusion.54
  18.0 1.5 collective-permute-start.7
  19.5 1.4 collective-permute-start.6
  21.0 1.5 fusion.55
  24.0 1.7 fusion.53
  27.1 1.7 collective-permute-start.2
  32.6 3.6 %collective-permute-start.10 = (bf16[32,1,1,4,2,2,128]{6,0,5,4,3,2,1:T(8,128)(2,1)}, bf16[32,1,1,4,2,2,128]{6,0,5,4,3,2,1:T(8,128)(2,1)S(1)}, u32[]{:S(2)}, u32[]{:S(2)}) collective-permute-start(bf16[32,1,1,4,2,2,128]{6,0,5,4,3,2,1:T(8,128)(2,1)} %get-tuple-element.23), channel_id=1, source_target_pairs={{8,0},{16,8},{24,16},{0,24},{9,1},{17,9},{25,17},{1,25},{10,2},{18... | collective-permute-start | bytes 393224 | tf_op jit(solution)/shard_map/ppermute | solution.py:24
  37.2 1.5 collective-permute-start.9
  41.1 2.5 %collective-permute-done.8 = bf16[32,1,1,1,2,2,128]{6,0,5,4,3,2,1:T(8,128)(2,1)S(1)} collective-permute-done((bf16[32,1,1,1,2,2,128]{6,0,5,4,3,2,1:T(8,128)(2,1)S(1)}, bf16[32,1,1,1,2,2,128]{6,0,5,4,3,2,1:T(8,128)(2,1)S(1)}, u32[]{:S(2)}, u32[]{:S(2)}) %collective-permute-start.8) | collective-permute-done | bytes 32800 | tf_op jit(solution)/shard_map/ppermute | solution.py:12
  48.6 38.6 %all-reduce.1 = (f32[32]{0:T(128)S(1)}, f32[32]{0:T(128)S(1)}) all-reduce(f32[32]{0:T(128)S(1)} %get-tuple-element.11, f32[32]{0:T(128)S(1)} %get-tuple-element.10), channel_id=1, replica_groups=mesh['ta'=4,'xyz'=8] {'ta','xyz'}, use_global_device_ids=true, to_apply=%region_1.2 | all-reduce | flops 64 | bytes 512 | tf_op jit(solution)/shard_map/psum | solution.py:104
  88.3 10.0 %all-gather.1 = bf16[8,48,32]{1,2,0:T(8,128)(2,1)S(1)} all-gather(bf16[1,48,32]{1,2,0:T(8,128)(2,1)S(1)} %fusion.22), channel_id=1, replica_groups=mesh['ta'=4,'xyz'=8] {'xyz'}, dimensions={0}, use_global_device_ids=true | all-gather | bytes 27648 | tf_op jit(solution)/shard_map/all_gather | solution.py:84
  99.0 2.1 %bitcast_dynamic-update-slice_fusion.2 = (bf16[32,1,9,1,4,2,2,128]{7,0,6,5,4,3,2,1:T(8,128)(2,1)S(1)}, bf16[32,1,1,4,2,2,128]{6,0,5,4,3,2,1:T(8,128)(2,1)}, f32[32,1,1,4,2,2,128]{6,0,5,4,3,2,1:T(8,128)}) fusion(bf16[1,1,4,2,2,48,128]{6,5,4,3,2,1,0:T(8,128)(2,1)} %param.6, bf16[384,32]{0,1:T(8,128)(2,1)} %reshape.332, bf16[1,48,384]{2,1,0:T(8,128)(2,1)} %param.7, ...), kind=kOutput, calls=%fused_computation.73 | convolution fusion | flops 7669247 | bytes 1044480 | tf_op jit(solution)/shard_map/tbzyxjk,nj->ntbzyxk/dot_general | solution.py:89
  103.0 1.5 collective-permute-start.13
  106.8 2.4 %collective-permute-start.18 = (bf16[32,1,1,4,1,2,128]{6,0,5,4,3,2,1:T(8,128)(2,1)S(1)}, bf16[32,1,1,4,1,2,128]{6,0,5,4,3,2,1:T(8,128)(2,1)S(1)}, u32[]{:S(2)}, u32[]{:S(2)}) collective-permute-start(bf16[32,1,1,4,1,2,128]{6,0,5,4,3,2,1:T(8,128)(2,1)S(1)} %get-tuple-element.36), channel_id=1, source_target_pairs={{0,6},{1,7},{2,0},{3,1},{4,2},{5,3},{6,4},{7,5},{8,14},{9,15},{10,... | collective-permute-start | bytes 196616 | tf_op jit(solution)/shard_map/ppermute | solution.py:12
  109.3 2.6 %collective-permute-start.14 = (bf16[32,1,1,4,2,1,128]{6,0,5,4,3,2,1:T(8,128)(2,1)S(1)}, bf16[32,1,1,4,2,1,128]{6,0,5,4,3,2,1:T(8,128)(2,1)S(1)}, u32[]{:S(2)}, u32[]{:S(2)}) collective-permute-start(bf16[32,1,1,4,2,1,128]{6,0,5,4,3,2,1:T(8,128)(2,1)S(1)} %get-tuple-element.38), channel_id=1, source_target_pairs={{0,7},{1,0},{2,1},{3,2},{4,3},{5,4},{6,5},{7,6},{8,15},{9,8},{10,9... | collective-permute-start | bytes 196616 | tf_op jit(solution)/shard_map/ppermute | solution.py:12
  111.9 2.7 %collective-permute-done.15 = bf16[32,1,1,4,2,1,128]{6,0,5,4,3,2,1:T(8,128)(2,1)S(1)} collective-permute-done((bf16[32,1,1,4,2,1,128]{6,0,5,4,3,2,1:T(8,128)(2,1)S(1)}, bf16[32,1,1,4,2,1,128]{6,0,5,4,3,2,1:T(8,128)(2,1)S(1)}, u32[]{:S(2)}, u32[]{:S(2)}) %collective-permute-start.15) | collective-permute-done | bytes 65568 | tf_op jit(solution)/shard_map/ppermute | solution.py:12
  114.5 2.2 %collective-permute-start.22 = (bf16[32,1,1,4,2,2,128]{6,0,5,4,3,2,1:T(8,128)(2,1)S(1)}, bf16[32,1,1,4,2,2,128]{6,0,5,4,3,2,1:T(8,128)(2,1)S(1)}, u32[]{:S(2)}, u32[]{:S(2)}) collective-permute-start(bf16[32,1,1,4,2,2,128]{6,0,5,4,3,2,1:T(8,128)(2,1)S(1)} %copy-done.5), channel_id=1, source_target_pairs={{8,0},{16,8},{24,16},{0,24},{9,1},{17,9},{25,17},{1,25},{10,2},{18... | collective-permute-start | bytes 393224 | tf_op jit(solution)/shard_map/ppermute | solution.py:24
  116.8 2.0 %collective-permute-start.23 = (bf16[32,1,1,4,2,2,128]{6,0,5,4,3,2,1:T(8,128)(2,1)S(1)}, bf16[32,1,1,4,2,2,128]{6,0,5,4,3,2,1:T(8,128)(2,1)S(1)}, u32[]{:S(2)}, u32[]{:S(2)}) collective-permute-start(bf16[32,1,1,4,2,2,128]{6,0,5,4,3,2,1:T(8,128)(2,1)S(1)} %copy-done.5), channel_id=1, source_target_pairs={{0,8},{8,16},{16,24},{24,0},{1,9},{9,17},{17,25},{25,1},{2,10},{10... | collective-permute-start | bytes 393224 | tf_op jit(solution)/shard_map/ppermute | solution.py:22
  121.9 3.1 %collective-permute-done.20 = bf16[32,1,1,1,2,2,128]{6,0,5,4,3,2,1:T(8,128)(2,1)S(1)} collective-permute-done((bf16[32,1,1,1,2,2,128]{6,0,5,4,3,2,1:T(8,128)(2,1)S(1)}, bf16[32,1,1,1,2,2,128]{6,0,5,4,3,2,1:T(8,128)(2,1)S(1)}, u32[]{:S(2)}, u32[]{:S(2)}) %collective-permute-start.20) | collective-permute-done | bytes 32800 | tf_op jit(solution)/shard_map/ppermute | solution.py:12
  130.0 12.8 %psum.44 = f32[32]{0:T(128)S(1)} all-reduce(f32[32]{0:T(128)S(1)} %multiply_reduce_fusion.2), channel_id=1, replica_groups=mesh['ta'=4,'xyz'=8] {'xyz'}, use_global_device_ids=true, to_apply=%region_5.6 | all-reduce | flops 32 | bytes 256 | tf_op jit(solution)/shard_map/psum | solution.py:117
  142.8 10.5 %psum.45 = f32[32]{0:T(128)S(1)} all-reduce(f32[32]{0:T(128)S(1)} %psum.44), channel_id=1, replica_groups=mesh['ta'=4,'xyz'=8] {'ta'}, use_global_device_ids=true, to_apply=%region_6.7 | all-reduce | flops 32 | bytes 256 | tf_op jit(solution)/shard_map/psum | solution.py:118
  154.2 37.6 %all-reduce = (f32[32]{0:T(128)S(1)}, f32[32]{0:T(128)S(1)}) all-reduce(f32[32]{0:T(128)S(1)} %get-tuple-element.9, f32[32]{0:T(128)S(1)} %get-tuple-element.8), channel_id=1, replica_groups=mesh['ta'=4,'xyz'=8] {'ta','xyz'}, use_global_device_ids=true, to_apply=%region_8.9 | all-reduce | flops 64 | bytes 512 | tf_op jit(solution)/shard_map/psum | solution.py:104
  (116 shorter events, 36.1 us)
Async XLA Ops:
  18.0 21.6 %collective-permute-start.7 = (bf16[32,1,1,4,1,2,128]{6,0,5,4,3,2,1:T(8,128)(2,1)}, bf16[32,1,1,4,1,2,128]{6,0,5,4,3,2,1:T(8,128)(2,1)}, u32[]{:S(2)}, u32[]{:S(2)}) collective-permute-start(bf16[32,1,1,4,1,2,128]{6,0,5,4,3,2,1:T(8,128)(2,1)} %get-tuple-element.44), channel_id=1, source_target_pairs={{0,2},{1,3},{2,4},{3,5},{4,6},{5,7},{6,0},{7,1},{8,10},{9,11},{10,... | collective-permute-start | bytes 196616 | tf_op jit(solution)/shard_map/ppermute | solution.py:12
  19.5 20.7 %collective-permute-start.6 = (bf16[32,1,1,4,1,2,128]{6,0,5,4,3,2,1:T(8,128)(2,1)}, bf16[32,1,1,4,1,2,128]{6,0,5,4,3,2,1:T(8,128)(2,1)}, u32[]{:S(2)}, u32[]{:S(2)}) collective-permute-start(bf16[32,1,1,4,1,2,128]{6,0,5,4,3,2,1:T(8,128)(2,1)} %get-tuple-element.44), channel_id=1, source_target_pairs={{0,6},{1,7},{2,0},{3,1},{4,2},{5,3},{6,4},{7,5},{8,14},{9,15},{10,... | collective-permute-start | bytes 196616 | tf_op jit(solution)/shard_map/ppermute | solution.py:12
  22.5 4.6 %collective-permute-start.1 = (bf16[32,1,1,4,2,1,128]{6,0,5,4,3,2,1:T(8,128)(2,1)}, bf16[32,1,1,4,2,1,128]{6,0,5,4,3,2,1:T(8,128)(2,1)}, u32[]{:S(2)}, u32[]{:S(2)}) collective-permute-start(bf16[32,1,1,4,2,1,128]{6,0,5,4,3,2,1:T(8,128)(2,1)} %get-tuple-element.47), channel_id=1, source_target_pairs={{0,7},{1,0},{2,1},{3,2},{4,3},{5,4},{6,5},{7,6},{8,15},{9,8},{10,9... | collective-permute-start | bytes 196616 | tf_op jit(solution)/shard_map/ppermute | solution.py:12
  22.5 6.3 %collective-permute-start = (bf16[32,1,1,4,2,1,128]{6,0,5,4,3,2,1:T(8,128)(2,1)}, bf16[32,1,1,4,2,1,128]{6,0,5,4,3,2,1:T(8,128)(2,1)}, u32[]{:S(2)}, u32[]{:S(2)}) collective-permute-start(bf16[32,1,1,4,2,1,128]{6,0,5,4,3,2,1:T(8,128)(2,1)} %get-tuple-element.47), channel_id=1, source_target_pairs={{0,1},{1,2},{2,3},{3,4},{4,5},{5,6},{6,7},{7,0},{8,9},{9,10},{10,1... | collective-permute-start | bytes 196616 | tf_op jit(solution)/shard_map/ppermute | solution.py:12
  23.0 8.5 %collective-permute-start.3 = (bf16[32,1,1,4,2,1,128]{6,0,5,4,3,2,1:T(8,128)(2,1)}, bf16[32,1,1,4,2,1,128]{6,0,5,4,3,2,1:T(8,128)(2,1)}, u32[]{:S(2)}, u32[]{:S(2)}) collective-permute-start(bf16[32,1,1,4,2,1,128]{6,0,5,4,3,2,1:T(8,128)(2,1)} %get-tuple-element.46), channel_id=1, source_target_pairs={{0,1},{1,2},{2,3},{3,4},{4,5},{5,6},{6,7},{7,0},{8,9},{9,10},{10,1... | collective-permute-start | bytes 196616 | tf_op jit(solution)/shard_map/ppermute | solution.py:12
  27.1 5.5 %collective-permute-start.2 = (bf16[32,1,1,4,2,1,128]{6,0,5,4,3,2,1:T(8,128)(2,1)}, bf16[32,1,1,4,2,1,128]{6,0,5,4,3,2,1:T(8,128)(2,1)S(1)}, u32[]{:S(2)}, u32[]{:S(2)}) collective-permute-start(bf16[32,1,1,4,2,1,128]{6,0,5,4,3,2,1:T(8,128)(2,1)} %get-tuple-element.46), channel_id=1, source_target_pairs={{0,7},{1,0},{2,1},{3,2},{4,3},{5,4},{6,5},{7,6},{8,15},{9,8},{10,9... | collective-permute-start | bytes 196616 | tf_op jit(solution)/shard_map/ppermute | solution.py:12
  28.8 8.3 %collective-permute-start.5 = (bf16[32,1,1,4,1,2,128]{6,0,5,4,3,2,1:T(8,128)(2,1)}, bf16[32,1,1,4,1,2,128]{6,0,5,4,3,2,1:T(8,128)(2,1)S(1)}, u32[]{:S(2)}, u32[]{:S(2)}) collective-permute-start(bf16[32,1,1,4,1,2,128]{6,0,5,4,3,2,1:T(8,128)(2,1)} %get-tuple-element.45), channel_id=1, source_target_pairs={{0,6},{1,7},{2,0},{3,1},{4,2},{5,3},{6,4},{7,5},{8,14},{9,15},{10,... | collective-permute-start | bytes 196616 | tf_op jit(solution)/shard_map/ppermute | solution.py:12
  31.5 5.7 %collective-permute-start.4 = (bf16[32,1,1,4,1,2,128]{6,0,5,4,3,2,1:T(8,128)(2,1)}, bf16[32,1,1,4,1,2,128]{6,0,5,4,3,2,1:T(8,128)(2,1)S(1)}, u32[]{:S(2)}, u32[]{:S(2)}) collective-permute-start(bf16[32,1,1,4,1,2,128]{6,0,5,4,3,2,1:T(8,128)(2,1)} %get-tuple-element.45), channel_id=1, source_target_pairs={{0,2},{1,3},{2,4},{3,5},{4,6},{5,7},{6,0},{7,1},{8,10},{9,11},{10,... | collective-permute-start | bytes 196616 | tf_op jit(solution)/shard_map/ppermute | solution.py:12
  32.6 11.1 %collective-permute-start.10 = (bf16[32,1,1,4,2,2,128]{6,0,5,4,3,2,1:T(8,128)(2,1)}, bf16[32,1,1,4,2,2,128]{6,0,5,4,3,2,1:T(8,128)(2,1)S(1)}, u32[]{:S(2)}, u32[]{:S(2)}) collective-permute-start(bf16[32,1,1,4,2,2,128]{6,0,5,4,3,2,1:T(8,128)(2,1)} %get-tuple-element.23), channel_id=1, source_target_pairs={{8,0},{16,8},{24,16},{0,24},{9,1},{17,9},{25,17},{1,25},{10,2},{18... | collective-permute-start | bytes 393224 | tf_op jit(solution)/shard_map/ppermute | solution.py:24
  37.1 7.1 %collective-permute-start.11 = (bf16[32,1,1,4,2,2,128]{6,0,5,4,3,2,1:T(8,128)(2,1)}, bf16[32,1,1,4,2,2,128]{6,0,5,4,3,2,1:T(8,128)(2,1)S(1)}, u32[]{:S(2)}, u32[]{:S(2)}) collective-permute-start(bf16[32,1,1,4,2,2,128]{6,0,5,4,3,2,1:T(8,128)(2,1)} %get-tuple-element.23), channel_id=1, source_target_pairs={{0,8},{8,16},{16,24},{24,0},{1,9},{9,17},{17,25},{25,1},{2,10},{10... | collective-permute-start | bytes 393224 | tf_op jit(solution)/shard_map/ppermute | solution.py:22
  37.2 6.5 %collective-permute-start.9 = (bf16[32,1,1,1,2,2,128]{6,0,5,4,3,2,1:T(8,128)(2,1)}, bf16[32,1,1,1,2,2,128]{6,0,5,4,3,2,1:T(8,128)(2,1)S(1)}, u32[]{:S(2)}, u32[]{:S(2)}) collective-permute-start(bf16[32,1,1,1,2,2,128]{6,0,5,4,3,2,1:T(8,128)(2,1)} %get-tuple-element.40), channel_id=1, source_target_pairs={{0,4},{1,5},{2,6},{3,7},{4,0},{5,1},{6,2},{7,3},{8,12},{9,13},{10,... | collective-permute-start | bytes 98312 | tf_op jit(solution)/shard_map/ppermute | solution.py:12
  39.6 4.0 %collective-permute-start.8 = (bf16[32,1,1,1,2,2,128]{6,0,5,4,3,2,1:T(8,128)(2,1)S(1)}, bf16[32,1,1,1,2,2,128]{6,0,5,4,3,2,1:T(8,128)(2,1)S(1)}, u32[]{:S(2)}, u32[]{:S(2)}) collective-permute-start(bf16[32,1,1,1,2,2,128]{6,0,5,4,3,2,1:T(8,128)(2,1)S(1)} %copy-done.10), channel_id=1, source_target_pairs={{0,4},{1,5},{2,6},{3,7},{4,0},{5,1},{6,2},{7,3},{8,12},{9,13},{10,... | collective-permute-start | bytes 98312 | tf_op jit(solution)/shard_map/ppermute | solution.py:12
  103.0 6.3 %collective-permute-start.13 = (bf16[32,1,1,4,2,1,128]{6,0,5,4,3,2,1:T(8,128)(2,1)S(1)}, bf16[32,1,1,4,2,1,128]{6,0,5,4,3,2,1:T(8,128)(2,1)S(1)}, u32[]{:S(2)}, u32[]{:S(2)}) collective-permute-start(bf16[32,1,1,4,2,1,128]{6,0,5,4,3,2,1:T(8,128)(2,1)S(1)} %get-tuple-element.39), channel_id=1, source_target_pairs={{0,7},{1,0},{2,1},{3,2},{4,3},{5,4},{6,5},{7,6},{8,15},{9,8},{10,9... | collective-permute-start | bytes 196616 | tf_op jit(solution)/shard_map/ppermute | solution.py:12
  104.4 7.4 %collective-permute-start.12 = (bf16[32,1,1,4,2,1,128]{6,0,5,4,3,2,1:T(8,128)(2,1)S(1)}, bf16[32,1,1,4,2,1,128]{6,0,5,4,3,2,1:T(8,128)(2,1)S(1)}, u32[]{:S(2)}, u32[]{:S(2)}) collective-permute-start(bf16[32,1,1,4,2,1,128]{6,0,5,4,3,2,1:T(8,128)(2,1)S(1)} %get-tuple-element.39), channel_id=1, source_target_pairs={{0,1},{1,2},{2,3},{3,4},{4,5},{5,6},{6,7},{7,0},{8,9},{9,10},{10,1... | collective-permute-start | bytes 196616 | tf_op jit(solution)/shard_map/ppermute | solution.py:12
  106.2 14.8 %collective-permute-start.19 = (bf16[32,1,1,4,1,2,128]{6,0,5,4,3,2,1:T(8,128)(2,1)S(1)}, bf16[32,1,1,4,1,2,128]{6,0,5,4,3,2,1:T(8,128)(2,1)S(1)}, u32[]{:S(2)}, u32[]{:S(2)}) collective-permute-start(bf16[32,1,1,4,1,2,128]{6,0,5,4,3,2,1:T(8,128)(2,1)S(1)} %get-tuple-element.36), channel_id=1, source_target_pairs={{0,2},{1,3},{2,4},{3,5},{4,6},{5,7},{6,0},{7,1},{8,10},{9,11},{10,... | collective-permute-start | bytes 196616 | tf_op jit(solution)/shard_map/ppermute | solution.py:12
  106.8 15.1 %collective-permute-start.18 = (bf16[32,1,1,4,1,2,128]{6,0,5,4,3,2,1:T(8,128)(2,1)S(1)}, bf16[32,1,1,4,1,2,128]{6,0,5,4,3,2,1:T(8,128)(2,1)S(1)}, u32[]{:S(2)}, u32[]{:S(2)}) collective-permute-start(bf16[32,1,1,4,1,2,128]{6,0,5,4,3,2,1:T(8,128)(2,1)S(1)} %get-tuple-element.36), channel_id=1, source_target_pairs={{0,6},{1,7},{2,0},{3,1},{4,2},{5,3},{6,4},{7,5},{8,14},{9,15},{10,... | collective-permute-start | bytes 196616 | tf_op jit(solution)/shard_map/ppermute | solution.py:12
  109.2 5.4 %collective-permute-start.15 = (bf16[32,1,1,4,2,1,128]{6,0,5,4,3,2,1:T(8,128)(2,1)S(1)}, bf16[32,1,1,4,2,1,128]{6,0,5,4,3,2,1:T(8,128)(2,1)S(1)}, u32[]{:S(2)}, u32[]{:S(2)}) collective-permute-start(bf16[32,1,1,4,2,1,128]{6,0,5,4,3,2,1:T(8,128)(2,1)S(1)} %get-tuple-element.38), channel_id=1, source_target_pairs={{0,1},{1,2},{2,3},{3,4},{4,5},{5,6},{6,7},{7,0},{8,9},{9,10},{10,1... | collective-permute-start | bytes 196616 | tf_op jit(solution)/shard_map/ppermute | solution.py:12
  109.3 5.3 %collective-permute-start.14 = (bf16[32,1,1,4,2,1,128]{6,0,5,4,3,2,1:T(8,128)(2,1)S(1)}, bf16[32,1,1,4,2,1,128]{6,0,5,4,3,2,1:T(8,128)(2,1)S(1)}, u32[]{:S(2)}, u32[]{:S(2)}) collective-permute-start(bf16[32,1,1,4,2,1,128]{6,0,5,4,3,2,1:T(8,128)(2,1)S(1)} %get-tuple-element.38), channel_id=1, source_target_pairs={{0,7},{1,0},{2,1},{3,2},{4,3},{5,4},{6,5},{7,6},{8,15},{9,8},{10,9... | collective-permute-start | bytes 196616 | tf_op jit(solution)/shard_map/ppermute | solution.py:12
  111.8 5.0 %collective-permute-start.17 = (bf16[32,1,1,4,1,2,128]{6,0,5,4,3,2,1:T(8,128)(2,1)S(1)}, bf16[32,1,1,4,1,2,128]{6,0,5,4,3,2,1:T(8,128)(2,1)S(1)}, u32[]{:S(2)}, u32[]{:S(2)}) collective-permute-start(bf16[32,1,1,4,1,2,128]{6,0,5,4,3,2,1:T(8,128)(2,1)S(1)} %get-tuple-element.37), channel_id=1, source_target_pairs={{0,6},{1,7},{2,0},{3,1},{4,2},{5,3},{6,4},{7,5},{8,14},{9,15},{10,... | collective-permute-start | bytes 196616 | tf_op jit(solution)/shard_map/ppermute | solution.py:12
  114.5 5.2 %collective-permute-start.16 = (bf16[32,1,1,4,1,2,128]{6,0,5,4,3,2,1:T(8,128)(2,1)S(1)}, bf16[32,1,1,4,1,2,128]{6,0,5,4,3,2,1:T(8,128)(2,1)S(1)}, u32[]{:S(2)}, u32[]{:S(2)}) collective-permute-start(bf16[32,1,1,4,1,2,128]{6,0,5,4,3,2,1:T(8,128)(2,1)S(1)} %get-tuple-element.37), channel_id=1, source_target_pairs={{0,2},{1,3},{2,4},{3,5},{4,6},{5,7},{6,0},{7,1},{8,10},{9,11},{10,... | collective-permute-start | bytes 196616 | tf_op jit(solution)/shard_map/ppermute | solution.py:12
  114.5 10.5 %collective-permute-start.22 = (bf16[32,1,1,4,2,2,128]{6,0,5,4,3,2,1:T(8,128)(2,1)S(1)}, bf16[32,1,1,4,2,2,128]{6,0,5,4,3,2,1:T(8,128)(2,1)S(1)}, u32[]{:S(2)}, u32[]{:S(2)}) collective-permute-start(bf16[32,1,1,4,2,2,128]{6,0,5,4,3,2,1:T(8,128)(2,1)S(1)} %copy-done.5), channel_id=1, source_target_pairs={{8,0},{16,8},{24,16},{0,24},{9,1},{17,9},{25,17},{1,25},{10,2},{18... | collective-permute-start | bytes 393224 | tf_op jit(solution)/shard_map/ppermute | solution.py:24
  116.8 8.3 %collective-permute-start.23 = (bf16[32,1,1,4,2,2,128]{6,0,5,4,3,2,1:T(8,128)(2,1)S(1)}, bf16[32,1,1,4,2,2,128]{6,0,5,4,3,2,1:T(8,128)(2,1)S(1)}, u32[]{:S(2)}, u32[]{:S(2)}) collective-permute-start(bf16[32,1,1,4,2,2,128]{6,0,5,4,3,2,1:T(8,128)(2,1)S(1)} %copy-done.5), channel_id=1, source_target_pairs={{0,8},{8,16},{16,24},{24,0},{1,9},{9,17},{17,25},{25,1},{2,10},{10... | collective-permute-start | bytes 393224 | tf_op jit(solution)/shard_map/ppermute | solution.py:22
  119.7 5.3 %collective-permute-start.21 = (bf16[32,1,1,1,2,2,128]{6,0,5,4,3,2,1:T(8,128)(2,1)S(1)}, bf16[32,1,1,1,2,2,128]{6,0,5,4,3,2,1:T(8,128)(2,1)S(1)}, u32[]{:S(2)}, u32[]{:S(2)}) collective-permute-start(bf16[32,1,1,1,2,2,128]{6,0,5,4,3,2,1:T(8,128)(2,1)S(1)} %get-tuple-element.32), channel_id=1, source_target_pairs={{0,4},{1,5},{2,6},{3,7},{4,0},{5,1},{6,2},{7,3},{8,12},{9,13},{10,... | collective-permute-start | bytes 98312 | tf_op jit(solution)/shard_map/ppermute | solution.py:12
  121.0 4.0 %collective-permute-start.20 = (bf16[32,1,1,1,2,2,128]{6,0,5,4,3,2,1:T(8,128)(2,1)S(1)}, bf16[32,1,1,1,2,2,128]{6,0,5,4,3,2,1:T(8,128)(2,1)S(1)}, u32[]{:S(2)}, u32[]{:S(2)}) collective-permute-start(bf16[32,1,1,1,2,2,128]{6,0,5,4,3,2,1:T(8,128)(2,1)S(1)} %get-tuple-element.33), channel_id=1, source_target_pairs={{0,4},{1,5},{2,6},{3,7},{4,0},{5,1},{6,2},{7,3},{8,12},{9,13},{10,... | collective-permute-start | bytes 98312 | tf_op jit(solution)/shard_map/ppermute | solution.py:12
  (11 other events, 236.4 us)
